TPU v7x, 128 devices: a whole 4x4x4 slice. The times are simulated.
128 devices in a mesh: segment: 4 (over x), dp: 32 (over y, z, core).
Axes of the slice: x: 4, y: 4, z: 4, core: 2. Of those that a mesh axis runs over, the one named last changes fastest.
Arguments:
- query_states: bfloat16 [1024, 32, 768], P('dp'), may hold values from -40 to 40
- passage_states: bfloat16 [512, 64, 768], P('dp'), may hold values from -40 to 40
- query_tokens: int32 [1024, 32], P('dp'), may hold values from 0 to 32099, as said below
- passage_tokens: int32 [512, 64], P('dp'), may hold values from 0 to 32099, as said below
- ff_gains: float32 [2, 768], replicated, may hold values from 0.1 to 1.9
- out_gains: float32 [2, 768], replicated, may hold values from 0.1 to 1.9
- w_gate: bfloat16 [2, 768, 2048], P(None, None, 'segment'), may hold values from -0.21875 to 0.21875
- w_up: bfloat16 [2, 768, 2048], P(None, None, 'segment'), may hold values from -0.21875 to 0.21875
- w_down: bfloat16 [2, 2048, 768], P(None, 'segment'), may hold values from -1 to 1
- w_proj: bfloat16 [2, 768, 768], replicated, may hold values from -0.21875 to 0.21875
- positive_ids: int32 [1024], P('dp'), may hold values from 0 to 511
- negative_ids: int32 [1024, 15], P('dp'), may hold values from 0 to 511
- negative_counts: int32 [1024], P('dp'), may hold values from 1 to 15, 7680 in all
Outputs:
- grad_gate: float32 [2, 768, 2048], P(None, 'dp', 'segment')
- grad_up: float32 [2, 768, 2048], P(None, 'dp', 'segment')
- grad_down: float32 [2, 2048, 768], P(None, 'segment', 'dp')
Inputs may be any that keep to these rules, and one draw needn't show every extreme that they name: `query_tokens`: each row holds token ids of 1 or more followed by zeros, at least 8 nonzero ids; the first row has no zeros. `passage_tokens`: each row holds token ids of 1 or more followed by zeros, at least 16 nonzero ids; the first row has no zeros. Only the first negative_counts[i] entries of row i are used; the counts sum to 7680.
All inputs are finite; a program needn't handle non-finite values. No bound on the sum of `negative_counts` on one device may be relied on, other than what follows from the above.
Results may differ from a plain program's by a relative error of at most 0.012.
Values may be sent and summed in bfloat16 or wider, within the bound.
No kernel may reach another device: no remote copies, remote signals or barrier semaphores. Data moves between devices by JAX's collectives and lax.ppermute only.
A program may use at most 128 MiB of HBM per device.

v0:
```python
import jax
import jax.numpy as jnp
from jax import lax
from jax.sharding import PartitionSpec as P

score_temp = 0.05
rank_temp = 1.0
recall_depth = 5.0
loss_scale = 16.0
norm_eps = 1e-06


def inverse_rms(values):
    return lax.rsqrt(jnp.mean(values * values, axis=-1, keepdims=True) + norm_eps)


def normed_input(states, ff_gain):
    widened = states.astype(jnp.float32)
    return (widened * inverse_rms(widened) * ff_gain).astype(jnp.bfloat16)


def pooled_embedding(summed, tokens, out_gain, proj_weight):
    normed = summed * inverse_rms(summed) * out_gain
    token_mask = (tokens != 0).astype(jnp.float32)[:, :, None]
    pooled = jnp.sum(normed * token_mask, axis=1) / jnp.sum(token_mask, axis=1)
    projected = jnp.dot(pooled, proj_weight.astype(jnp.float32), precision=lax.Precision.HIGHEST)
    return projected * lax.rsqrt(jnp.sum(projected * projected, axis=-1, keepdims=True) + norm_eps)


def recall_loss(scores, valid_mask):
    margins = (scores[:, 1:] - scores[:, :1]) / score_temp
    soft_ranks = 1.0 + jnp.sum(jax.nn.sigmoid(margins) * valid_mask, axis=1)
    return loss_scale * jnp.sum(jax.nn.sigmoid((soft_ranks - recall_depth - 0.5) / rank_temp))


def contract(left, right):
    return lax.dot_general(
        left, right, (((0,), (0,)), ((), ())), preferred_element_type=jnp.float32
    )


def natural_order(gathered, segments, groups, per_device):
    model_width = gathered.shape[-1]
    shaped = gathered.reshape(segments, groups, per_device, model_width)
    return jnp.transpose(shaped, (1, 0, 2, 3)).reshape(-1, model_width)


def score_grads_of(scores, counts):
    slots = scores.shape[1] - 1
    valid_mask = (
        lax.broadcasted_iota(jnp.int32, (scores.shape[0], slots), 1) < counts[:, None]
    ).astype(jnp.float32)
    return jax.grad(recall_loss)(scores, valid_mask)


def body(
    query_states,
    passage_states,
    query_tokens,
    passage_tokens,
    ff_gains,
    out_gains,
    w_gate,
    w_up,
    w_down,
    w_proj,
    positive_ids,
    negative_ids,
    negative_counts,
):
    segments = lax.axis_size("segment")
    groups = lax.axis_size("dp")
    segment_index = lax.axis_index("segment")
    model_width = query_states.shape[-1]
    query_dev = query_states.shape[0] // segments
    passage_dev = passage_states.shape[0] // segments

    def forward_part(states, tower_index):
        normed = normed_input(states, ff_gains[tower_index]).reshape(-1, model_width)
        gate_pre = jnp.dot(normed, w_gate[tower_index], preferred_element_type=jnp.float32)
        up_pre = jnp.dot(normed, w_up[tower_index], preferred_element_type=jnp.float32)
        activated, gelu_back = jax.vjp(jax.nn.gelu, gate_pre)
        hidden = (activated * up_pre).astype(jnp.bfloat16)
        branch = jnp.dot(hidden, w_down[tower_index], preferred_element_type=jnp.float32).reshape(
            states.shape
        )
        return (normed, up_pre, activated, gelu_back, hidden, branch)

    def own_rows(values, per_device):
        return lax.dynamic_slice_in_dim(values, segment_index * per_device, per_device, 0)

    def head_of(tokens, tower_index):
        return lambda summed: pooled_embedding(
            summed, tokens, out_gains[tower_index], w_proj[tower_index]
        )

    query_parts = forward_part(query_states, 0)
    passage_parts = forward_part(passage_states, 1)
    query_branch, passage_branch = (
        lax.psum_scatter(query_parts[5], "segment", scatter_dimension=0, tiled=True),
        lax.psum_scatter(passage_parts[5], "segment", scatter_dimension=0, tiled=True),
    )
    query_embed, query_back = jax.vjp(
        head_of(own_rows(query_tokens, query_dev), 0),
        own_rows(query_states, query_dev).astype(jnp.float32) + query_branch,
    )
    passage_embed, passage_back = jax.vjp(
        head_of(own_rows(passage_tokens, passage_dev), 1),
        own_rows(passage_states, passage_dev).astype(jnp.float32) + passage_branch,
    )
    query_round = query_embed.astype(jnp.bfloat16)
    passage_round = passage_embed.astype(jnp.bfloat16)
    id_radix = 256
    own_ids = jnp.concatenate(
        [own_rows(positive_ids, query_dev)[:, None], own_rows(negative_ids, query_dev)], axis=1
    )
    slots = own_ids.shape[1]
    own_meta = jnp.concatenate(
        [own_ids // id_radix, own_ids % id_radix, own_rows(negative_counts, query_dev)[:, None]],
        axis=1,
    ).astype(jnp.bfloat16)
    meta_width = own_meta.shape[1]
    meta_rows = -(-query_dev * meta_width // model_width)
    meta_flat = jnp.pad(
        own_meta.reshape(-1), (0, meta_rows * model_width - query_dev * meta_width)
    ).reshape(meta_rows, model_width)
    packed = jnp.concatenate([query_round, passage_round, meta_flat], axis=0)
    gathered = lax.all_gather(packed, ("dp", "segment"), axis=0, tiled=False)
    gathered = gathered.reshape(groups, segments, -1, model_width)
    query_all = gathered[:, :, :query_dev].reshape(-1, model_width)
    passage_all = gathered[:, :, query_dev : query_dev + passage_dev].reshape(-1, model_width)
    meta_all = (
        gathered[:, :, query_dev + passage_dev :]
        .reshape(groups, segments, -1)[:, :, : query_dev * meta_width]
        .reshape(-1, meta_width)
        .astype(jnp.int32)
    )
    cand_all = meta_all[:, :slots] * id_radix + meta_all[:, slots : 2 * slots]
    counts_all = meta_all[:, 2 * slots]
    passage_total = passage_all.shape[0]
    all_scores = lax.dot_general(
        query_all, passage_all, (((1,), (1,)), ((), ())), preferred_element_type=jnp.float32
    )
    scores = jnp.take_along_axis(all_scores, cand_all, axis=1)
    score_grads = score_grads_of(scores, counts_all)
    dp_index = lax.axis_index("dp")
    query_start = (dp_index * segments + segment_index) * query_dev
    passage_start = (dp_index * segments + segment_index) * passage_dev
    own_cand = lax.dynamic_slice_in_dim(cand_all, query_start, query_dev, 0)
    own_grads = lax.dynamic_slice_in_dim(score_grads, query_start, query_dev, 0)
    every_id = lax.broadcasted_iota(jnp.int32, (1, 1, passage_total), 2)
    query_coef = jnp.sum(
        jnp.where(own_cand[:, :, None] == every_id, own_grads[:, :, None], 0.0), axis=1
    )
    own_passages = passage_start + lax.broadcasted_iota(jnp.int32, (1, 1, passage_dev), 2)
    passage_coef = jnp.sum(
        jnp.where(cand_all[:, :, None] == own_passages, score_grads[:, :, None], 0.0), axis=1
    )
    query_grad = jnp.dot(
        query_coef, passage_all.astype(jnp.float32), precision=lax.Precision.HIGHEST
    )
    passage_grad = lax.dot_general(
        passage_coef,
        query_all.astype(jnp.float32),
        (((0,), (0,)), ((), ())),
        precision=lax.Precision.HIGHEST,
        preferred_element_type=jnp.float32,
    )
    query_share = query_back(query_grad)[0].astype(jnp.bfloat16)
    passage_share = passage_back(passage_grad)[0].astype(jnp.bfloat16)
    query_rows, passage_rows = (
        lax.all_gather(query_share, "segment", axis=0, tiled=True),
        lax.all_gather(passage_share, "segment", axis=0, tiled=True),
    )

    def backward_part(tower_parts, row_grads, tower_index):
        normed, up_pre, activated, gelu_back, hidden, branch = tower_parts
        flat_grad = row_grads.reshape(-1, model_width)
        hidden_grad = lax.dot_general(
            flat_grad,
            w_down[tower_index],
            (((1,), (1,)), ((), ())),
            preferred_element_type=jnp.float32,
        )
        gate_grad = gelu_back(hidden_grad * up_pre)[0].astype(jnp.bfloat16)
        up_grad = (hidden_grad * activated).astype(jnp.bfloat16)
        return (normed, gate_grad, up_grad, hidden, flat_grad)

    towers_back = (
        backward_part(query_parts, query_rows, 0),
        backward_part(passage_parts, passage_rows, 1),
    )

    def weight_terms():
        matrices = [[], [], []]
        for normed, gate_grad, up_grad, hidden, flat_grad in towers_back:
            matrices[0].append(contract(normed, gate_grad))
            matrices[1].append(contract(normed, up_grad))
            matrices[2].append(contract(flat_grad, hidden))
        return jnp.stack([jnp.stack(pieces, axis=1) for pieces in matrices], axis=1)

    summed_grads = lax.psum_scatter(weight_terms(), "dp", scatter_dimension=0, tiled=True)
    grad_gate = jnp.transpose(summed_grads[:, 0], (1, 0, 2))
    grad_up = jnp.transpose(summed_grads[:, 1], (1, 0, 2))
    grad_down = jnp.transpose(summed_grads[:, 2], (1, 2, 0))
    return (grad_gate, grad_up, grad_down)


def solution(mesh):
    return jax.shard_map(
        body,
        mesh=mesh,
        in_specs=(
            P("dp", None, None),
            P("dp", None, None),
            P("dp", None),
            P("dp", None),
            P(),
            P(),
            P(None, None, "segment"),
            P(None, None, "segment"),
            P(None, "segment", None),
            P(),
            P("dp"),
            P("dp", None),
            P("dp"),
        ),
        out_specs=(P(None, "dp", "segment"), P(None, "dp", "segment"), P(None, "segment", "dp")),
        check_vma=False,
    )
```

profile of v0, /device:TPU:0, one launch (start us, length us, event | category | flops | bytes accessed | tf_op | source)
XLA Modules:
  0.0 496.1 jit_solution(10540428919395859232)
XLA Ops:
  7.2 0.8 slice_reduce_fusion.5
  8.1 1.9 fusion
  10.5 1.0 fusion.56
  12.5 2.6 multiply_convert_fusion.3
  15.1 1.0 copy-done.18
  16.1 2.6 fusion.50
  18.8 1.3 copy-done.4
  21.5 1.0 fusion.48
  22.9 2.6 multiply_convert_fusion.2
  25.6 1.0 copy-done.19
  26.5 2.6 fusion.42
  32.3 27.3 %reduce-scatter.4.cloned.1.call-done = f32[8,32,768]{2,1,0:T(8,128)} async-done(((f32[32,32,768]{2,1,0:T(8,128)}), f32[8,32,768]{2,1,0:T(8,128)}) %reduce-scatter.4.cloned.1.call-update) | async-done | bytes 786448 | tf_op jit(solution)/shard_map/reduce_scatter | solution.py:100
  59.6 1.5 multiply_reduce_fusion.5
  61.1 1.4 multiply_reduce_fusion.4
  63.4 36.7 %reduce-scatter.6.cloned.1.call-done = f32[4,64,768]{2,1,0:T(8,128)} async-done(((f32[16,64,768]{2,1,0:T(8,128)}), f32[4,64,768]{2,1,0:T(8,128)}) %reduce-scatter.6.cloned.1.call-update) | async-done | bytes 786448 | tf_op jit(solution)/shard_map/reduce_scatter | solution.py:101
  100.0 1.5 multiply_reduce_fusion.3
  101.6 1.4 multiply_reduce_fusion.2
  105.3 65.5 %all-gather.10.cloned.1.call-done = bf16[128,13,768]{2,1,0:T(8,128)(2,1)} async-done(((bf16[1,13,768]{2,1,0:T(8,128)(2,1)}), bf16[128,13,768]{2,1,0:T(8,128)(2,1)}) %all-gather.10.cloned.1.call-update) | async-done | bytes 2555920 | tf_op jit(solution)/shard_map/all_gather | solution.py:128
  170.8 1.8 slice.100
  173.2 1.0 slice_reduce_fusion.1
  174.1 1.0 bitcast_or_fusion
  175.2 1.6 slice.106
  176.8 1.3 slice.105
  178.5 0.9 copy-done.9
  179.4 2.4 fusion.121
  181.8 129.5 %gather_fusion = f32[16384]{0:T(1024)S(1)} fusion(f32[1024,512]{1,0:T(8,128)S(1)} %fusion.121, s32[16384]{0:T(1024)S(1)} %reshape.165), kind=kCustom, calls=%fused_computation | custom fusion | bytes 262144 | tf_op jit(solution)/shard_map/jit(take_along_axis)/gather | solution.py:144
  312.6 1.0 fusion.115
  313.6 1.0 copy.42
  315.6 1.7 multiply_reduce_fusion.6
  317.3 2.3 fusion.28
  320.0 1.0 fusion.40
  321.3 1.3 pad_add_fusion
  322.9 2.4 multiply_reduce_fusion.8
  325.4 2.3 fusion.31
  328.1 1.1 fusion.41
  329.5 15.6 %all-gather.6.cloned.1.call-done = bf16[32,32,768]{2,1,0:T(8,128)(2,1)} async-done(((bf16[8,32,768]{2,1,0:T(8,128)(2,1)}), bf16[32,32,768]{2,1,0:T(8,128)(2,1)}) %all-gather.6.cloned.1.call-update) | async-done | bytes 1572880 | tf_op jit(solution)/shard_map/all_gather | solution.py:172
  345.0 2.9 convolution_bitcast_fusion.1
  347.9 2.3 fusion.52
  350.3 22.7 %all-gather.8.cloned.1.call-done = bf16[16,64,768]{2,1,0:T(8,128)(2,1)} async-done(((bf16[4,64,768]{2,1,0:T(8,128)(2,1)}), bf16[16,64,768]{2,1,0:T(8,128)(2,1)}) %all-gather.8.cloned.1.call-update) | async-done | bytes 1572880 | tf_op jit(solution)/shard_map/all_gather | solution.py:173
  373.0 2.8 convolution_bitcast_fusion
  375.9 1.0 fusion.44
  377.9 1.1 convolution_bitcast_fusion.3
  379.5 2.4 convolution_bitcast_fusion.5
  381.9 1.1 convolution_bitcast_fusion.2
  383.5 2.4 convolution_bitcast_fusion.4
  386.8 4.8 pad_maximum_fusion
  391.7 95.9 %reduce-scatter.8.cloned.1.call-done = f32[24,3,2,512]{3,0,2,1:T(8,128)} async-done(((f32[768,3,2,512]{3,0,2,1:T(8,128)}), f32[24,3,2,512]{3,0,2,1:T(8,128)}) %reduce-scatter.8.cloned.1.call-update) | async-done | bytes 294928 | tf_op jit(solution)/shard_map/reduce_scatter | solution.py:202
  487.5 1.7 slice_bitcast_fusion
  (205 shorter events, 16.8 us)
Async XLA Ops:
  7.2 23.0 %copy-start = (s32[32,15]{0,1:T(8,128)S(1)}, s32[32,15]{0,1:T(8,128)}, u32[]{:S(2)}) copy-start(s32[32,15]{0,1:T(8,128)} %param.24) | copy-start | bytes 5764
  7.2 52.4 %reduce-scatter.4.cloned.1.call-start = ((), (), s32[]{:S(2)}) async-start(), calls=%async_computation.3 | async-start | bytes 3932160 | tf_op jit(solution)/shard_map/reduce_scatter | solution.py:100
  12.5 3.6 copy-start.11
  18.7 81.3 %reduce-scatter.6.cloned.1.call-start = ((), (), s32[]{:S(2)}) async-start(), calls=%async_computation.4 | async-start | bytes 3932160 | tf_op jit(solution)/shard_map/reduce_scatter | solution.py:101
  22.9 3.6 copy-start.12
  29.2 3.0 copy-start.41
  29.2 141.6 %all-gather.10.cloned.1.call-start = ((), (), s32[]{:S(2)}) async-start(), calls=%async_computation.8 | async-start | bytes 3170304 | tf_op jit(solution)/shard_map/all_gather | solution.py:128
  31.4 70.2 %copy-start.35 = (f32[4,64]{1,0:T(4,128)}, f32[4,64]{1,0:T(4,128)S(1)}, u32[]{:S(2)}) copy-start(f32[4,64]{1,0:T(4,128)S(1)} %get-tuple-element.14) | copy-start | bytes 3076
  31.4 71.6 %copy-start.46 = (f32[4]{0:T(128)}, f32[4]{0:T(128)S(1)}, u32[]{:S(2)}) copy-start(f32[4]{0:T(128)S(1)} %get-tuple-element.13) | copy-start | bytes 52
  32.2 69.3 %copy-start.26 = (f32[8,32]{1,0:T(8,128)}, f32[8,32]{1,0:T(8,128)S(1)}, u32[]{:S(2)}) copy-start(f32[8,32]{1,0:T(8,128)S(1)} %get-tuple-element.12) | copy-start | bytes 3076
  32.2 69.3 %copy-start.50 = (f32[8]{0:T(128)}, f32[8]{0:T(128)S(1)}, u32[]{:S(2)}) copy-start(f32[8]{0:T(128)S(1)} %get-tuple-element.11) | copy-start | bytes 100
  32.3 69.3 %copy-start.24 = (f32[768]{0:T(1024)}, f32[768]{0:T(1024)S(1)}, u32[]{:S(2)}) copy-start(f32[768]{0:T(1024)S(1)} %get-tuple-element.5) | copy-start | bytes 9220
  32.3 69.3 %copy-start.22 = (f32[768]{0:T(1024)}, f32[768]{0:T(1024)S(1)}, u32[]{:S(2)}) copy-start(f32[768]{0:T(1024)S(1)} %get-tuple-element.6) | copy-start | bytes 9220
  59.6 3.0 copy-start.52
  63.3 109.3 %copy-start.20 = (f32[8,768]{1,0:T(8,128)}, f32[8,768]{1,0:T(8,128)S(1)}, u32[]{:S(2)}) copy-start(f32[8,768]{1,0:T(8,128)S(1)} %get-tuple-element.27) | copy-start | bytes 73732
  63.3 109.3 %copy-start.62 = (f32[8]{0:T(128)}, f32[8]{0:T(128)S(1)}, u32[]{:S(2)}) copy-start(f32[8]{0:T(128)S(1)} %get-tuple-element.26) | copy-start | bytes 100
  63.4 109.3 %copy-start.42 = (f32[8]{0:T(128)}, f32[8]{0:T(128)S(1)}, u32[]{:S(2)}) copy-start(f32[8]{0:T(128)S(1)} %add_rsqrt_fusion.3) | copy-start | bytes 100
  100.0 3.0 copy-start.53
  101.5 71.2 %copy-start.39 = (f32[4,64]{1,0:T(4,128)}, f32[4,64]{1,0:T(4,128)S(1)}, u32[]{:S(2)}) copy-start(f32[4,64]{1,0:T(4,128)S(1)} %multiply_reduce_fusion.3) | copy-start | bytes 3076
  101.6 71.2 %copy-start.37 = (f32[4,64]{1,0:T(4,128)}, f32[4,64]{1,0:T(4,128)S(1)}, u32[]{:S(2)}) copy-start(f32[4,64]{1,0:T(4,128)S(1)} %fusion.94) | copy-start | bytes 3076
  103.8 69.0 %copy-start.48 = (f32[4]{0:T(128)}, f32[4]{0:T(128)S(1)}, u32[]{:S(2)}) copy-start(f32[4]{0:T(128)S(1)} %add_rsqrt_fusion.2) | copy-start | bytes 52
  105.1 240.0 %all-gather.6.cloned.1.call-start = ((), (), s32[]{:S(2)}) async-start(), calls=%async_computation.5 | async-start | bytes 1966080 | tf_op jit(solution)/shard_map/all_gather | solution.py:172
  173.2 3.6 copy-start.10
  181.8 129.7 %copy-start.8 = (s32[1024,16]{1,0:T(8,128)S(1)}, s32[1024,16]{1,0:T(8,128)}, u32[]{:S(2)}) copy-start(s32[1024,16]{1,0:T(8,128)} %get-tuple-element.10) | copy-start | bytes 196612
  311.6 3.9 copy-start.21
  312.0 5.3 %copy-start.63 = (f32[8]{0:T(128)S(1)}, f32[8]{0:T(128)}, u32[]{:S(2)}) copy-start(f32[8]{0:T(128)} %copy-done.62) | copy-start | bytes 100
  312.0 5.3 %copy-start.43 = (f32[8]{0:T(128)S(1)}, f32[8]{0:T(128)}, u32[]{:S(2)}) copy-start(f32[8]{0:T(128)} %copy-done.42) | copy-start | bytes 100
  312.0 5.3 %copy-start.51 = (f32[8]{0:T(128)S(1)}, f32[8]{0:T(128)}, u32[]{:S(2)}) copy-start(f32[8]{0:T(128)} %copy-done.50) | copy-start | bytes 100
  313.6 6.0 %copy-start.3 = (bf16[32,32,768]{2,1,0:T(8,128)(2,1)S(1)}, bf16[32,32,768]{2,1,0:T(8,128)(2,1)}, u32[]{:S(2)}) copy-start(bf16[32,32,768]{2,1,0:T(8,128)(2,1)} %param.13) | copy-start | bytes 4718596
  313.6 6.0 %copy-start.6 = (f32[8,32,768]{2,1,0:T(8,128)S(1)}, f32[8,32,768]{2,1,0:T(8,128)}, u32[]{:S(2)}) copy-start(f32[8,32,768]{2,1,0:T(8,128)} %reduce-scatter.4.cloned.1.call-done) | copy-start | bytes 2359300
  313.6 6.0 %copy-start.25 = (f32[768]{0:T(1024)S(1)}, f32[768]{0:T(1024)}, u32[]{:S(2)}) copy-start(f32[768]{0:T(1024)} %copy-done.24) | copy-start | bytes 9220
  313.6 6.0 %copy-start.27 = (f32[8,32]{1,0:T(8,128)S(1)}, f32[8,32]{1,0:T(8,128)}, u32[]{:S(2)}) copy-start(f32[8,32]{1,0:T(8,128)} %copy-done.26) | copy-start | bytes 3076
  314.7 5.3 %copy-start.34 = (f32[8,32]{1,0:T(8,128)S(1)}, f32[8,32]{1,0:T(8,128)}, u32[]{:S(2)}) copy-start(f32[8,32]{1,0:T(8,128)} %copy-done.33) | copy-start | bytes 3076
  314.7 5.3 %copy-start.32 = (f32[8,32]{1,0:T(8,128)S(1)}, f32[8,32]{1,0:T(8,128)}, u32[]{:S(2)}) copy-start(f32[8,32]{1,0:T(8,128)} %copy-done.31) | copy-start | bytes 3076
  320.0 2.9 copy-start.29
  321.1 51.9 %all-gather.8.cloned.1.call-start = ((), (), s32[]{:S(2)}) async-start(), calls=%async_computation.6 | async-start | bytes 1966080 | tf_op jit(solution)/shard_map/all_gather | solution.py:173
  321.3 4.1 copy-start.61
  321.3 4.1 copy-start.47
  321.3 4.1 copy-start.49
  322.6 5.1 %copy-start.5 = (bf16[16,64,768]{2,1,0:T(8,128)(2,1)S(1)}, bf16[16,64,768]{2,1,0:T(8,128)(2,1)}, u32[]{:S(2)}) copy-start(bf16[16,64,768]{2,1,0:T(8,128)(2,1)} %param.14) | copy-start | bytes 4718596
  322.6 5.1 %copy-start.7 = (f32[4,64,768]{2,1,0:T(8,128)S(1)}, f32[4,64,768]{2,1,0:T(8,128)}, u32[]{:S(2)}) copy-start(f32[4,64,768]{2,1,0:T(8,128)} %reduce-scatter.6.cloned.1.call-done) | copy-start | bytes 2359300
  322.6 5.2 %copy-start.23 = (f32[768]{0:T(1024)S(1)}, f32[768]{0:T(1024)}, u32[]{:S(2)}) copy-start(f32[768]{0:T(1024)} %copy-done.22) | copy-start | bytes 9220
  322.6 5.2 %copy-start.36 = (f32[4,64]{1,0:T(4,128)S(1)}, f32[4,64]{1,0:T(4,128)}, u32[]{:S(2)}) copy-start(f32[4,64]{1,0:T(4,128)} %copy-done.35) | copy-start | bytes 3076
  322.8 5.3 %copy-start.40 = (f32[4,64]{1,0:T(4,128)S(1)}, f32[4,64]{1,0:T(4,128)}, u32[]{:S(2)}) copy-start(f32[4,64]{1,0:T(4,128)} %copy-done.39) | copy-start | bytes 3076
  322.9 5.2 %copy-start.38 = (f32[4,64]{1,0:T(4,128)S(1)}, f32[4,64]{1,0:T(4,128)}, u32[]{:S(2)}) copy-start(f32[4,64]{1,0:T(4,128)} %copy-done.37) | copy-start | bytes 3076
  329.2 158.4 %reduce-scatter.8.cloned.1.call-start = ((), (), s32[]{:S(2)}) async-start(), calls=%async_computation.7 | async-start | bytes 9732096 | tf_op jit(solution)/shard_map/reduce_scatter | solution.py:202
  373.0 3.9 copy-start.66
  391.7 97.6 %copy-start.1 = (s32[32,15]{0,1:T(8,128)S(1)}, s32[32,15]{0,1:T(8,128)}, u32[]{:S(2)}) copy-start(s32[32,15]{0,1:T(8,128)} %param.24) | copy-start | bytes 5764
  (29 other events, 48.4 us)
Sparse Core Ops, SparseCore 0:
  18.8 40.7 reduce-scatter.3
  62.0 37.9 reduce-scatter.5
  105.2 65.5 all-gather.9
  321.2 23.8 all-gather.5
  346.6 26.3 all-gather.7
  391.8 95.7 reduce-scatter.7
where the time goes:
time: 497 us; the launch traced here: 496 us
  waiting for transfers between devices  264 us (53%)
  local copies, waits for them, and re-layouts  150 us (30%)
  matrix products  41.1 us (8%)
  other arithmetic  25.1 us (5%)
  between operations  15.2 us (3%)
    gather x3, local copies, waits for them, and re-layouts, body(): scores = jnp.take_along_axis(all_scores, cand_all, axis=1)  130 us
    reduce_scatter x1, waiting for transfers between devices, body(): lax.psum_scatter(weight_terms(), 'dp', scatter_dimension=0, tiled=True)  95.9 us
    all_gather x1, waiting for transfers between devices, body(): gathered = lax.all_gather(packed, ('dp', 'segment'), axis=0, tiled=False)  65.5 us
    reduce_scatter x1, waiting for transfers between devices, body(): lax.psum_scatter(passage_parts[5], 'segment', scatter_dimension=0, tiled=...  36.7 us
    reduce_scatter x1, waiting for transfers between devices, body(): lax.psum_scatter(query_parts[5], 'segment', scatter_dimension=0, tiled=True)  27.3 us
    all_gather x1, waiting for transfers between devices, body(): lax.all_gather(passage_share, 'segment', axis=0, tiled=True)  22.7 us
    all_gather x1, waiting for transfers between devices, body(): lax.all_gather(query_share, 'segment', axis=0, tiled=True)  15.6 us
    dot_general x6, matrix products, contract(): lax.dot_general(left, right, (((0,), (0,)), ((), ())), preferred_element_...  12.7 us
  transfers between devices with their start and end apart: 6, of which 6 were waited for; matrix products, arithmetic and copies ran while one was open for 5% of the time, Pallas kernels for 0%

commit v1 on v0

--- a/solution.py
+++ b/solution.py
@@ -1,3 +1,4 @@
+import functools
 import jax
 import jax.numpy as jnp
 from jax import lax
@@ -8,6 +9,38 @@
 recall_depth = 5.0
 loss_scale = 16.0
 norm_eps = 1e-06
+
+
+def _derive_sums_all(mat, group_axis, join_dim):
+    low, r_now, b_next = (
+        lax.axis_size(group_axis),
+        lax.axis_index(group_axis),
+        mat.shape[join_dim],
+    )
+    column = []
+    for k0 in tuple(range(low)):
+        column.append((k0, (k0 + 1) % low))
+    buffers = []
+    for k0 in [*range(low)]:
+        buffers.append((k0, (k0 - 1) % low))
+    w_next = jnp.zeros((*mat.shape[:join_dim], low * b_next, *mat.shape[join_dim + 1 :]), mat.dtype)
+    w_next = lax.dynamic_update_slice_in_dim(w_next, mat, r_now * b_next, axis=join_dim)
+    current_value = everything = mat
+    carry_out = low // 2
+    for d in [*range(1, carry_out + 1)]:
+        current_value = lax.ppermute(current_value, group_axis, column)
+        w_next = lax.dynamic_update_slice_in_dim(
+            w_next, current_value, (r_now - d) % low * b_next, axis=join_dim
+        )
+        if d < low - carry_out:
+            everything = lax.ppermute(everything, group_axis, buffers)
+            w_next = lax.dynamic_update_slice_in_dim(
+                w_next, everything, (r_now + d) % low * b_next, axis=join_dim
+            )
+    return w_next
+
+
+results_reach = functools.partial(_derive_sums_all, group_axis="segment", join_dim=0)
 
 
 def inverse_rms(values):
@@ -169,7 +202,7 @@
     query_share = query_back(query_grad)[0].astype(jnp.bfloat16)
     passage_share = passage_back(passage_grad)[0].astype(jnp.bfloat16)
     query_rows, passage_rows = (
-        lax.all_gather(query_share, "segment", axis=0, tiled=True),
+        results_reach(query_share),
         lax.all_gather(passage_share, "segment", axis=0, tiled=True),
     )
 

time: 497 us -> 478 us (0.962)
  waiting for transfers between devices: 264 us -> 236 us
  local copies, waits for them, and re-layouts: 150 us -> 159 us
    all_gather x1, waiting for transfers between devices: 22.7 us -> 0.01 us  [body(): lax.all_gather(passage_share, 'segment', axis=0, tiled=True)]
    ppermute x0 -> x3, waiting for transfers between devices: none -> 17.6 us  [the longest x2 17.6 us: _derive_sums_all(): current_value = lax.ppermute(current_value, group_axis, column)]
    all_gather x1 -> x0, waiting for transfers between devices: 15.6 us -> none  [body(): lax.all_gather(query_share, 'segment', axis=0, tiled=True)]
    reduce_scatter x1, waiting for transfers between devices: 95.9 us -> 89.7 us  [body(): lax.psum_scatter(weight_terms(), 'dp', scatter_dimension=0, tiled=True)]
    unnamed x143 -> x155, local copies, waits for them, and re-layouts: 9.62 us -> 12.1 us
  transfers between devices with their start and end apart: 6 -> 8, of which waited for: 6 -> 6; matrix products, arithmetic and copies ran while one was open for 5% -> 7% of each run, Pallas kernels for 0% -> 0%
where the time goes in v1:
time: 478 us
  waiting for transfers between devices  236 us (49%)
  local copies, waits for them, and re-layouts  159 us (33%)
  matrix products  40.6 us (8%)
  other arithmetic  23.1 us (5%)
  between operations  14.9 us (3%)
    gather x3, local copies, waits for them, and re-layouts, body(): scores = jnp.take_along_axis(all_scores, cand_all, axis=1)  130 us
    reduce_scatter x1, waiting for transfers between devices, body(): lax.psum_scatter(weight_terms(), 'dp', scatter_dimension=0, tiled=True)  89.7 us
    all_gather x1, waiting for transfers between devices, body(): gathered = lax.all_gather(packed, ('dp', 'segment'), axis=0, tiled=False)  65 us
    reduce_scatter x1, waiting for transfers between devices, body(): lax.psum_scatter(passage_parts[5], 'segment', scatter_dimension=0, tiled=...  36.7 us
    reduce_scatter x1, waiting for transfers between devices, body(): lax.psum_scatter(query_parts[5], 'segment', scatter_dimension=0, tiled=True)  27.3 us
    ppermute x2, waiting for transfers between devices, _derive_sums_all(): current_value = lax.ppermute(current_value, group_axis, column)  17.6 us
    dot_general x6, matrix products, contract(): lax.dot_general(left, right, (((0,), (0,)), ((), ())), preferred_element_...  14.5 us
    unnamed x155, local copies, waits for them, and re-layouts  12.1 us
  transfers between devices with their start and end apart: 8, of which 6 were waited for; matrix products, arithmetic and copies ran while one was open for 7% of the time, Pallas kernels for 0%

profile of v1, /device:TPU:0, one launch (start us, length us, event | category | flops | bytes accessed | tf_op | source)
XLA Modules:
  0.0 477.6 jit_solution(2228618564687936686)
XLA Ops:
  8.1 1.9 fusion
  10.5 1.0 fusion.56
  12.5 2.6 multiply_convert_fusion.3
  15.1 1.0 copy-done.22
  16.1 2.6 fusion.50
  18.8 1.3 copy-done.4
  21.5 1.0 fusion.48
  22.9 2.7 multiply_convert_fusion.2
  25.6 1.0 copy-done.23
  26.6 2.7 fusion.42
  32.3 27.3 %reduce-scatter.4.cloned.1.call-done = f32[8,32,768]{2,1,0:T(8,128)} async-done(((f32[32,32,768]{2,1,0:T(8,128)}), f32[8,32,768]{2,1,0:T(8,128)}) %reduce-scatter.4.cloned.1.call-update) | async-done | bytes 786448 | tf_op jit(solution)/shard_map/reduce_scatter | solution.py:133
  59.6 1.5 multiply_reduce_fusion.5
  61.1 1.4 multiply_reduce_fusion.4
  63.4 36.7 %reduce-scatter.6.cloned.1.call-done = f32[4,64,768]{2,1,0:T(8,128)} async-done(((f32[16,64,768]{2,1,0:T(8,128)}), f32[4,64,768]{2,1,0:T(8,128)}) %reduce-scatter.6.cloned.1.call-update) | async-done | bytes 786448 | tf_op jit(solution)/shard_map/reduce_scatter | solution.py:134
  100.0 1.5 multiply_reduce_fusion.3
  101.6 1.4 multiply_reduce_fusion.2
  105.8 65.0 %all-gather.7.cloned.1.call-done = bf16[128,13,768]{2,1,0:T(8,128)(2,1)} async-done(((bf16[1,13,768]{2,1,0:T(8,128)(2,1)}), bf16[128,13,768]{2,1,0:T(8,128)(2,1)}) %all-gather.7.cloned.1.call-update) | async-done | bytes 2555920 | tf_op jit(solution)/shard_map/all_gather | solution.py:161
  170.8 1.8 slice.100
  173.2 0.9 slice_reduce_fusion.1
  174.4 1.8 slice.106
  176.2 1.3 slice.105
  180.2 2.4 fusion.123
  182.7 129.5 %gather_fusion = f32[16384]{0:T(1024)S(1)} fusion(f32[1024,512]{1,0:T(8,128)S(1)} %fusion.123, s32[16384]{0:T(1024)S(1)} %reshape.165), kind=kCustom, calls=%fused_computation | custom fusion | bytes 262144 | tf_op jit(solution)/shard_map/jit(take_along_axis)/gather | solution.py:177
  313.5 1.0 fusion.117
  316.4 1.0 fusion.28
  317.9 1.3 broadcast_in_dim.77
  319.2 1.1 constant_dynamic-update-slice_fusion.3
  320.6 3.0 collective-permute-start.1
  323.9 2.2 multiply_reduce_fusion.8
  326.2 2.3 fusion.31
  328.9 1.0 fusion.41
  330.0 2.9 collective-permute-done
  332.9 1.8 constant_dynamic-update-slice_fusion.2
  334.7 1.8 constant_dynamic-update-slice_fusion.1
  336.5 14.7 %collective-permute-done.2 = bf16[8,32,768]{2,1,0:T(8,128)(2,1)S(1)} collective-permute-done((bf16[8,32,768]{2,1,0:T(8,128)(2,1)}, bf16[8,32,768]{2,1,0:T(8,128)(2,1)S(1)}, u32[]{:S(2)}, u32[]{:S(2)}) %collective-permute-start.2) | collective-permute-done | bytes 393248 | tf_op jit(solution)/shard_map/ppermute | solution.py:31
  352.0 2.8 convolution_bitcast_fusion.1
  354.9 2.6 fusion.52
  357.5 2.3 convolution_bitcast_fusion.3
  359.8 3.1 convolution_bitcast_fusion.5
  362.9 2.8 convolution_bitcast_fusion
  365.7 1.0 fusion.44
  367.8 1.1 convolution_bitcast_fusion.2
  369.4 2.4 convolution_bitcast_fusion.4
  372.1 1.1 copy-done.21
  373.5 1.1 copy-done.20
  374.9 4.8 pad_maximum_fusion
  379.7 89.7 %reduce-scatter.8.cloned.1.call-done = f32[24,3,2,512]{3,0,2,1:T(8,128)} async-done(((f32[768,3,2,512]{3,0,2,1:T(8,128)}), f32[24,3,2,512]{3,0,2,1:T(8,128)}) %reduce-scatter.8.cloned.1.call-update) | async-done | bytes 294928 | tf_op jit(solution)/shard_map/reduce_scatter | solution.py:235
  469.3 1.7 slice_bitcast_fusion
  (224 shorter events, 21.9 us)
Async XLA Ops:
  7.2 23.0 %copy-start = (s32[32,15]{0,1:T(8,128)S(1)}, s32[32,15]{0,1:T(8,128)}, u32[]{:S(2)}) copy-start(s32[32,15]{0,1:T(8,128)} %param.24) | copy-start | bytes 5764
  7.2 2.8 copy-start.2
  7.2 52.4 %reduce-scatter.4.cloned.1.call-start = ((), (), s32[]{:S(2)}) async-start(), calls=%async_computation.3 | async-start | bytes 3932160 | tf_op jit(solution)/shard_map/reduce_scatter | solution.py:133
  12.5 3.6 copy-start.13
  18.7 81.3 %reduce-scatter.6.cloned.1.call-start = ((), (), s32[]{:S(2)}) async-start(), calls=%async_computation.4 | async-start | bytes 3932160 | tf_op jit(solution)/shard_map/reduce_scatter | solution.py:134
  22.9 2.7 copy-start.73
  22.9 3.7 copy-start.14
  29.2 3.0 copy-start.47
  29.3 141.5 %all-gather.7.cloned.1.call-start = ((), (), s32[]{:S(2)}) async-start(), calls=%async_computation.7 | async-start | bytes 3170304 | tf_op jit(solution)/shard_map/all_gather | solution.py:161
  31.4 70.1 %copy-start.40 = (f32[4,64]{1,0:T(4,128)}, f32[4,64]{1,0:T(4,128)S(1)}, u32[]{:S(2)}) copy-start(f32[4,64]{1,0:T(4,128)S(1)} %get-tuple-element.16) | copy-start | bytes 3076
  31.4 71.6 %copy-start.53 = (f32[4]{0:T(128)}, f32[4]{0:T(128)S(1)}, u32[]{:S(2)}) copy-start(f32[4]{0:T(128)S(1)} %get-tuple-element.15) | copy-start | bytes 52
  32.2 69.3 %copy-start.31 = (f32[8,32]{1,0:T(8,128)}, f32[8,32]{1,0:T(8,128)S(1)}, u32[]{:S(2)}) copy-start(f32[8,32]{1,0:T(8,128)S(1)} %get-tuple-element.14) | copy-start | bytes 3076
  32.2 69.3 %copy-start.57 = (f32[8]{0:T(128)}, f32[8]{0:T(128)S(1)}, u32[]{:S(2)}) copy-start(f32[8]{0:T(128)S(1)} %get-tuple-element.13) | copy-start | bytes 100
  32.3 69.2 %copy-start.29 = (f32[768]{0:T(1024)}, f32[768]{0:T(1024)S(1)}, u32[]{:S(2)}) copy-start(f32[768]{0:T(1024)S(1)} %get-tuple-element.5) | copy-start | bytes 9220
  32.3 69.3 %copy-start.27 = (f32[768]{0:T(1024)}, f32[768]{0:T(1024)S(1)}, u32[]{:S(2)}) copy-start(f32[768]{0:T(1024)S(1)} %get-tuple-element.6) | copy-start | bytes 9220
  59.6 3.0 copy-start.59
  63.3 109.3 %copy-start.25 = (f32[8,768]{1,0:T(8,128)}, f32[8,768]{1,0:T(8,128)S(1)}, u32[]{:S(2)}) copy-start(f32[8,768]{1,0:T(8,128)S(1)} %get-tuple-element.29) | copy-start | bytes 73732
  63.3 109.3 %copy-start.69 = (f32[8]{0:T(128)}, f32[8]{0:T(128)S(1)}, u32[]{:S(2)}) copy-start(f32[8]{0:T(128)S(1)} %get-tuple-element.28) | copy-start | bytes 100
  63.3 109.3 %copy-start.48 = (f32[8]{0:T(128)}, f32[8]{0:T(128)S(1)}, u32[]{:S(2)}) copy-start(f32[8]{0:T(128)S(1)} %add_rsqrt_fusion.3) | copy-start | bytes 100
  100.0 3.0 copy-start.60
  101.5 71.2 %copy-start.44 = (f32[4,64]{1,0:T(4,128)}, f32[4,64]{1,0:T(4,128)S(1)}, u32[]{:S(2)}) copy-start(f32[4,64]{1,0:T(4,128)S(1)} %multiply_reduce_fusion.3) | copy-start | bytes 3076
  101.5 71.2 %copy-start.42 = (f32[4,64]{1,0:T(4,128)}, f32[4,64]{1,0:T(4,128)S(1)}, u32[]{:S(2)}) copy-start(f32[4,64]{1,0:T(4,128)S(1)} %fusion.95) | copy-start | bytes 3076
  103.8 69.0 %copy-start.55 = (f32[4]{0:T(128)}, f32[4]{0:T(128)S(1)}, u32[]{:S(2)}) copy-start(f32[4]{0:T(128)S(1)} %add_rsqrt_fusion.2) | copy-start | bytes 52
  105.1 257.8 %all-gather.5.cloned.1.call-start = ((), (), s32[]{:S(2)}) async-start(), calls=%async_computation.5 | async-start | bytes 1966080 | tf_op jit(solution)/shard_map/all_gather | solution.py:206
  173.1 3.1 copy-start.12
  174.4 4.2 copy-start.8
  182.6 129.7 %copy-start.9 = (s32[1024,16]{1,0:T(8,128)S(1)}, s32[1024,16]{1,0:T(8,128)}, u32[]{:S(2)}) copy-start(s32[1024,16]{1,0:T(8,128)} %copy-done.8) | copy-start | bytes 196612
  314.8 3.0 copy-start.39
  315.8 3.4 copy-start.37
  317.8 5.9 %copy-start.24 = (s32[1024,16]{0,1:T(8,128)S(1)}, s32[1024,16]{0,1:T(8,128)}, u32[]{:S(2)}) copy-start(s32[1024,16]{0,1:T(8,128)} %copy.43) | copy-start | bytes 196612
  317.8 5.9 %copy-start.50 = (s32[4]{0:T(128)S(1)}, s32[4]{0:T(128)}, u32[]{:S(2)}) copy-start(s32[4]{0:T(128)} %iota_add_fusion) | copy-start | bytes 52
  317.8 6.0 %copy-start.34 = (f32[4,768]{1,0:T(4,128)S(1)}, f32[4,768]{1,0:T(4,128)}, u32[]{:S(2)}) copy-start(f32[4,768]{1,0:T(4,128)} %copy-done.33) | copy-start | bytes 36868
  319.2 7.0 %copy-start.68 = (f32[4]{0:T(128)S(1)}, f32[4]{0:T(128)}, u32[]{:S(2)}) copy-start(f32[4]{0:T(128)} %copy-done.67) | copy-start | bytes 52
  319.2 7.0 %copy-start.54 = (f32[4]{0:T(128)S(1)}, f32[4]{0:T(128)}, u32[]{:S(2)}) copy-start(f32[4]{0:T(128)} %copy-done.53) | copy-start | bytes 52
  319.2 7.0 %copy-start.56 = (f32[4]{0:T(128)S(1)}, f32[4]{0:T(128)}, u32[]{:S(2)}) copy-start(f32[4]{0:T(128)} %copy-done.55) | copy-start | bytes 52
  320.3 8.2 %copy-start.5 = (bf16[16,64,768]{2,1,0:T(8,128)(2,1)S(1)}, bf16[16,64,768]{2,1,0:T(8,128)(2,1)}, u32[]{:S(2)}) copy-start(bf16[16,64,768]{2,1,0:T(8,128)(2,1)} %param.14) | copy-start | bytes 4718596
  320.3 8.3 %copy-start.7 = (f32[4,64,768]{2,1,0:T(8,128)S(1)}, f32[4,64,768]{2,1,0:T(8,128)}, u32[]{:S(2)}) copy-start(f32[4,64,768]{2,1,0:T(8,128)} %reduce-scatter.6.cloned.1.call-done) | copy-start | bytes 2359300
  320.3 8.3 %copy-start.28 = (f32[768]{0:T(1024)S(1)}, f32[768]{0:T(1024)}, u32[]{:S(2)}) copy-start(f32[768]{0:T(1024)} %copy-done.27) | copy-start | bytes 9220
  320.3 8.3 %copy-start.41 = (f32[4,64]{1,0:T(4,128)S(1)}, f32[4,64]{1,0:T(4,128)}, u32[]{:S(2)}) copy-start(f32[4,64]{1,0:T(4,128)} %copy-done.40) | copy-start | bytes 3076
  320.3 12.6 %collective-permute-start = (bf16[8,32,768]{2,1,0:T(8,128)(2,1)S(1)}, bf16[8,32,768]{2,1,0:T(8,128)(2,1)}, u32[]{:S(2)}, u32[]{:S(2)}) collective-permute-start(bf16[8,32,768]{2,1,0:T(8,128)(2,1)S(1)} %get-tuple-element.8), channel_id=1, source_target_pairs={{0,32},{32,64},{64,96},{96,0},{1,33},{33,65},{65,97},{97,1},{2,34}... | collective-permute-start | bytes 1179656 | tf_op jit(solution)/shard_map/ppermute | solution.py:31
  320.6 14.1 %collective-permute-start.1 = (bf16[8,32,768]{2,1,0:T(8,128)(2,1)S(1)}, bf16[8,32,768]{2,1,0:T(8,128)(2,1)}, u32[]{:S(2)}, u32[]{:S(2)}) collective-permute-start(bf16[8,32,768]{2,1,0:T(8,128)(2,1)S(1)} %get-tuple-element.8), channel_id=1, source_target_pairs={{0,96},{32,0},{64,32},{96,64},{1,97},{33,1},{65,33},{97,65},{2,98}... | collective-permute-start | bytes 1179656 | tf_op jit(solution)/shard_map/ppermute | solution.py:36
  323.7 5.1 %copy-start.45 = (f32[4,64]{1,0:T(4,128)S(1)}, f32[4,64]{1,0:T(4,128)}, u32[]{:S(2)}) copy-start(f32[4,64]{1,0:T(4,128)} %copy-done.44) | copy-start | bytes 3076
  323.9 5.0 %copy-start.43 = (f32[4,64]{1,0:T(4,128)S(1)}, f32[4,64]{1,0:T(4,128)}, u32[]{:S(2)}) copy-start(f32[4,64]{1,0:T(4,128)} %copy-done.42) | copy-start | bytes 3076
  330.0 139.4 %reduce-scatter.8.cloned.1.call-start = ((), (), s32[]{:S(2)}) async-start(), calls=%async_computation.6 | async-start | bytes 9732096 | tf_op jit(solution)/shard_map/reduce_scatter | solution.py:235
  332.9 18.3 %collective-permute-start.2 = (bf16[8,32,768]{2,1,0:T(8,128)(2,1)}, bf16[8,32,768]{2,1,0:T(8,128)(2,1)S(1)}, u32[]{:S(2)}, u32[]{:S(2)}) collective-permute-start(bf16[8,32,768]{2,1,0:T(8,128)(2,1)} %collective-permute-done), channel_id=1, source_target_pairs={{0,32},{32,64},{64,96},{96,0},{1,33},{33,65},{65,97},{97,1},{2,34}... | collective-permute-start | bytes 1179656 | tf_op jit(solution)/shard_map/ppermute | solution.py:31
  352.0 2.9 copy-start.15
  362.9 2.8 copy-start.66
  379.7 91.4 %copy-start.1 = (s32[32,15]{0,1:T(8,128)S(1)}, s32[32,15]{0,1:T(8,128)}, u32[]{:S(2)}) copy-start(s32[32,15]{0,1:T(8,128)} %param.24) | copy-start | bytes 5764
  (37 other events, 59.5 us)
Sparse Core Ops, SparseCore 0:
  18.8 40.7 reduce-scatter.3
  62.0 37.9 reduce-scatter.5
  105.2 65.5 all-gather.6
  330.1 27.5 all-gather.4
  379.8 89.5 reduce-scatter.7
